TPU v7x, 128 devices: a whole 4x4x4 slice. The times are simulated.
128 devices in a mesh: seq: 16 (over x_hi, z, core), kvh: 8 (over x_lo, y).
Axes of the slice: x: 4 (x_hi: 2, x_lo: 2; x = x_hi * 2 + x_lo), y: 4, z: 4, core: 2. Of those that a mesh axis runs over, the one named last changes fastest.
Arguments:
- normed: bfloat16 [4096, 4096], P('seq'), may hold values from -8 to 8
- w_query: bfloat16 [4096, 4096], P(None, 'kvh'), may hold values from -1 to 1, as said below
- w_key: bfloat16 [4096, 1024], P(None, 'kvh'), may hold values from -1 to 1, as said below
- w_value: bfloat16 [4096, 1024], P(None, 'kvh'), may hold values from -0.09375 to 0.09375
- positions: int32 [4096], P('seq'), may hold values from 0 to 4222, as said below
- block_mask: int32 [32, 32], P('seq'), may hold values from 0 to 1, as said below
- grad_attn: bfloat16 [4096, 4096], P('seq', 'kvh'), may hold values from -6 to 6
Outputs:
- grad_normed: bfloat16 [4096, 4096], P('seq', 'kvh')
- grad_wq: float32 [4096, 4096], P('seq', 'kvh')
- grad_wk: float32 [4096, 1024], P('seq', 'kvh')
- grad_wv: float32 [4096, 1024], P('seq', 'kvh')
Inputs may be any that keep to these rules, and one draw needn't show every extreme that they name: Within a block positions rise by one per token; block b starts between b * 128 and (b + 1) * 128 - 1, block 0 at 0, the last block at its latest start. `block_mask`: the diagonal is 1; a block may read only blocks of earlier rounds besides itself; entries for earlier rounds are 0 or 1. `w_query`: entries of about 4096^(-1/2) in size. `w_key`: entries of about 4096^(-1/2) in size.
All inputs are finite; a program needn't handle non-finite values.
Results may differ from a plain program's by a relative error of at most 0.019.
The roundings to bfloat16 on the way count: a program that leaves them out, or rounds other values in their place, can miss the bound.
Values may be sent and summed in bfloat16 or wider, within the bound.
No kernel may reach another device: no remote copies, remote signals or barrier semaphores. Data moves between devices by JAX's collectives and lax.ppermute only.
A program may use at most 128 MiB of HBM per device.

v0:
```python
import jax
import jax.numpy as jnp
from jax import lax
from jax.sharding import PartitionSpec as P

HEAD = 128
BLOCK = 128
THETA = 500000.0


def rotate(values, positions, rotation_sign):
    tok_rows = values.shape[0]
    head_count = values.shape[1] // HEAD
    half_size = HEAD // 2
    pieces = values.reshape(tok_rows, head_count, HEAD)
    frequency = THETA ** (-(jnp.arange(half_size, dtype=jnp.float32) * (2.0 / HEAD)))
    angles = positions.astype(jnp.float32)[:, None] * frequency[None, :]
    cosine = jnp.cos(angles)[:, None, :]
    sine_part = rotation_sign * jnp.sin(angles)[:, None, :]
    lower_half = pieces[:, :, :half_size]
    upper_half = pieces[:, :, half_size:]
    turned = jnp.concatenate(
        [
            lower_half * cosine - upper_half * sine_part,
            upper_half * cosine + lower_half * sine_part,
        ],
        axis=2,
    )
    return turned.reshape(tok_rows, head_count * HEAD)


def visible(mask_table, query_block0, query_count, key_count):
    query_local = jnp.arange(query_count)
    key_local = jnp.arange(key_count)
    query_block = query_block0 + query_local // BLOCK
    key_block = key_local // BLOCK
    allowed = jnp.repeat(jnp.repeat(mask_table, BLOCK, axis=0), BLOCK, axis=1) == 1
    inner_ok = (key_local % BLOCK)[None, :] <= (query_local % BLOCK)[:, None]
    return allowed & ((query_block[:, None] != key_block[None, :]) | inner_ok)


def product(form, left, right):
    return jnp.einsum(form, left, right, preferred_element_type=jnp.float32)


def masked_scores(queries, keys, seen):
    scores = product("tgd,sd->gts", queries, keys) * HEAD ** (-0.5)
    return jnp.where(seen[None], scores, -1e30)


def softmax_stats(queries, keys, values, grad_heads, seen):
    scores = masked_scores(queries, keys, seen)
    row_max = jnp.max(scores, axis=2, keepdims=True)
    log_total = row_max[:, :, 0] + jnp.log(jnp.sum(jnp.exp(scores - row_max), axis=2))
    weights = jnp.where(seen[None], jnp.exp(scores - log_total[:, :, None]), 0.0).astype(
        jnp.bfloat16
    )
    outputs = product("gts,sd->gtd", weights, values)
    row_dots = jnp.sum(outputs * jnp.transpose(grad_heads.astype(jnp.float32), (1, 0, 2)), axis=2)
    return (log_total, row_dots)


def attention_grads(queries, keys, values, grad_heads, seen, log_total, row_dots):
    scores = masked_scores(queries, keys, seen)
    probs = jnp.where(seen[None], jnp.exp(scores - log_total[:, :, None]), 0.0)
    weights = probs.astype(jnp.bfloat16)
    grad_probs = product("tgd,sd->gts", grad_heads, values)
    grad_scores = (probs * (grad_probs - row_dots[:, :, None]) * HEAD ** (-0.5)).astype(
        jnp.bfloat16
    )
    grad_query = product("gts,sd->tgd", grad_scores, keys)
    grad_key = product("gts,tgd->sd", grad_scores, queries)
    grad_value = product("gts,tgd->sd", weights, grad_heads)
    return (grad_query, grad_key, grad_value)


def body(normed, w_query, w_key, w_value, positions, block_mask, grad_attn):
    tok_rows = normed.shape[0]
    group_size = w_query.shape[1] // w_key.shape[1]
    width_query = group_size * HEAD
    blk_local = tok_rows // BLOCK
    my_index = lax.axis_index("seq")
    queries = rotate(
        jnp.dot(normed, w_query, preferred_element_type=jnp.float32), positions, 1.0
    ).astype(jnp.bfloat16)
    keys = rotate(
        jnp.dot(normed, w_key, preferred_element_type=jnp.float32), positions, 1.0
    ).astype(jnp.bfloat16)
    values = jnp.dot(normed, w_value, preferred_element_type=jnp.float32).astype(jnp.bfloat16)
    keys_all, values_all = (
        lax.all_gather(keys, "seq", axis=0, tiled=True),
        lax.all_gather(values, "seq", axis=0, tiled=True),
    )
    seen = visible(block_mask, my_index * blk_local, tok_rows, keys_all.shape[0])
    total_parts = []
    dots_parts = []
    query_heads = queries.reshape(tok_rows, group_size, HEAD)
    grad_heads = grad_attn.reshape(tok_rows, group_size, HEAD)
    log_total, row_dots = softmax_stats(query_heads, keys_all, values_all, grad_heads, seen)
    grad_query, grad_key, grad_value = attention_grads(
        query_heads, keys_all, values_all, grad_heads, seen, log_total, row_dots
    )
    query_parts = grad_query.reshape(tok_rows, width_query)
    total_parts.append(log_total.T)
    dots_parts.append(row_dots.T)
    key_total, value_total = (
        lax.psum_scatter(
            grad_key.astype(jnp.bfloat16), "seq", scatter_dimension=0, tiled=True
        ).astype(jnp.float32),
        lax.psum_scatter(
            grad_value.astype(jnp.bfloat16), "seq", scatter_dimension=0, tiled=True
        ).astype(jnp.float32),
    )
    query_grad = rotate(query_parts, positions, -1.0).astype(jnp.bfloat16)
    key_grad = rotate(key_total, positions, -1.0).astype(jnp.bfloat16)
    value_grad = value_total.astype(jnp.bfloat16)
    joined = jnp.concatenate([query_grad, key_grad, value_grad], axis=1)
    weight_grads = lax.psum_scatter(
        lax.dot_general(
            normed, joined, (((0,), (0,)), ((), ())), preferred_element_type=jnp.float32
        ).astype(jnp.bfloat16),
        "seq",
        scatter_dimension=0,
        tiled=True,
    ).astype(jnp.float32)
    query_cols = query_grad.shape[1]
    key_cols = key_grad.shape[1]
    grad_wq = weight_grads[:, :query_cols]
    grad_wk = weight_grads[:, query_cols : query_cols + key_cols]
    grad_wv = weight_grads[:, query_cols + key_cols :]
    contract = (((1,), (1,)), ((), ()))
    partial_input = lax.dot_general(
        query_grad, w_query, contract, preferred_element_type=jnp.float32
    )
    partial_input = partial_input + lax.dot_general(
        key_grad, w_key, contract, preferred_element_type=jnp.float32
    )
    partial_input = partial_input + lax.dot_general(
        value_grad, w_value, contract, preferred_element_type=jnp.float32
    )
    grad_normed = lax.psum_scatter(
        partial_input.astype(jnp.bfloat16), "kvh", scatter_dimension=1, tiled=True
    )
    return (grad_normed, grad_wq, grad_wk, grad_wv)


def solution(mesh):
    in_specs = (
        P("seq", None),
        P(None, "kvh"),
        P(None, "kvh"),
        P(None, "kvh"),
        P("seq"),
        P("seq", None),
        P("seq", "kvh"),
    )
    out_specs = (P("seq", "kvh"), P("seq", "kvh"), P("seq", "kvh"), P("seq", "kvh"))
    return jax.shard_map(body, mesh=mesh, in_specs=in_specs, out_specs=out_specs, check_vma=False)
```

profile of v0, /device:TPU:0, one launch (start us, length us, event | category | flops | bytes accessed | tf_op | source)
XLA Modules:
  0.0 413.1 jit_solution(13094747481903445248)
XLA Ops:
  7.2 0.0 copy-start
  7.2 0.0 all-gather.6.cloned.1.call-start
  7.2 0.8 convert_element_type.52
  8.1 0.7 copy-done
  8.8 2.1 convolution_bitcast_fusion.3
  10.9 0.3 fusion.34
  11.2 0.6 pad_maximum_fusion.2
  11.8 0.0 all-gather.6.cloned.1.call-update
  11.9 0.0 all-gather.4.cloned.1.call-start
  11.9 2.5 convolution_convert_fusion.1
  14.5 0.0 all-gather.4.cloned.1.call-update
  14.5 0.0 reduce-scatter.5.cloned.1.call-start
  14.5 1.2 broadcast_multiply_fusion
  15.8 0.6 fusion.37
  16.4 3.4 fusion.55
  19.8 0.2 reshape.293
  20.0 1.1 fusion.53
  21.1 0.6 and_select_fusion
  21.7 0.7 broadcast_compare_fusion
  22.4 0.1 copy.27
  22.5 0.1 broadcast_in_dim.30
  22.6 0.6 copy.63
  23.2 0.8 copy.31
  24.1 1.9 subtract_convert_fusion.1
  26.0 2.5 bitcast_and_fusion
  28.5 28.9 %all-gather.6.cloned.1.call-done = bf16[4096,1,128]{0,2,1:T(8,128)(2,1)} async-done(((bf16[256,1,128]{0,2,1:T(8,128)(2,1)}), bf16[4096,1,128]{0,2,1:T(8,128)(2,1)}) %all-gather.6.cloned.1.call-update) | async-done | bytes 1048592 | tf_op jit(solution)/shard_map/all_gather | solution.py:91
  57.4 4.5 %fusion.4 = (f32[4,256]{1,0:T(4,128)S(1)}, f32[4096,256,4]{1,0,2:T(8,128)S(1)}) fusion(pred[256,4096]{0,1:T(8,128)(4,1)S(1)} %bitcast_and_fusion, bf16[256,4,64]{2,0,1:T(8,128)(2,1)} %get-tuple-element.13, bf16[256,4,64]{2,0,1:T(8,128)(2,1)S(1)} %get-tuple-element.12, bf16[4096,1,128]{0,2,1:T(8,128)(2,1)} %all-gather.6.cloned.1.call-done), kind=kOutput, calls=%fused_computation.8 | convolution fusion | flops 1086848000 | bytes 19140608 | tf_op jit(solution)/shard_map/tgd,sd->gts/dot_general | solution.py:43
  61.9 3.7 exponential_reduce_fusion
  65.5 2.1 copy-done.2
  67.6 37.1 %all-gather.4.cloned.1.call-done = bf16[4096,128]{1,0:T(8,128)(2,1)} async-done(((bf16[256,128]{1,0:T(8,128)(2,1)}), bf16[4096,128]{1,0:T(8,128)(2,1)}) %all-gather.4.cloned.1.call-update) | async-done | bytes 1048592 | tf_op jit(solution)/shard_map/all_gather | solution.py:92
  104.7 10.0 %fusion.9 = f32[4,256]{1,0:T(4,128)S(1)} fusion(bf16[4096,128]{1,0:T(8,128)(2,1)} %all-gather.4.cloned.1.call-done, bf16[256,4,128]{0,2,1:T(8,128)(2,1)} %bitcast.86, f32[4096,256,4]{1,0,2:T(8,128)} %copy-done.2, f32[4,256]{1,0:T(4,128)S(1)} %log_add_fusion, pred[256,4096]{0,1:T(8,128)(4,1)S(1)} %bitcast_and_fusion), kind=kOutput, calls=%fused_computation.21 | convolution fusion | flops 1095105536 | bytes 19144704 | tf_op jit(solution)/shard_map/gts,sd->gtd/dot_general | solution.py:43
  114.7 0.0 copy-start.4
  114.7 9.6 %fusion.2 = bf16[4,256,4096]{1,2,0:T(8,128)(2,1)S(1)} fusion(f32[4096,256,4]{1,0,2:T(8,128)} %copy-done.2, bf16[256,4,128]{0,2,1:T(8,128)(2,1)S(1)} %bitcast.88, f32[4,256]{1,0:T(4,128)S(1)} %fusion.9, f32[4,256]{1,0:T(4,128)S(1)} %log_add_fusion, pred[256,4096]{0,1:T(8,128)(4,1)S(1)} %bitcast_and_fusion, bf16[4096,128]{1,0:T(8,128)(2,1)S(1)} %copy-done.13), kind=kOutput, calls=%fused_computation.3 | convolution fusion | flops 1107296256 | bytes 27533312 | tf_op jit(solution)/shard_map/tgd,sd->gts/dot_general | solution.py:43
  124.4 3.2 copy-done.1
  127.6 3.9 fusion.7
  131.5 0.0 reduce-scatter.5.cloned.1.call-update
  131.5 0.3 reduce-scatter.7.cloned.1.call-start
  131.8 11.4 %fusion.8 = bf16[4096,128]{1,0:T(8,128)(2,1)} fusion(bf16[256,4,128]{0,2,1:T(8,128)(2,1)} %bitcast.87, f32[4096,256,4]{1,0,2:T(8,128)} %copy-done.2, f32[4,256]{1,0:T(4,128)S(1)} %log_add_fusion, pred[256,4096]{0,1:T(8,128)(4,1)S(1)} %bitcast_and_fusion), kind=kOutput, calls=%fused_computation.17 | convolution fusion | flops 1095237632 | bytes 19140608 | tf_op jit(solution)/shard_map/gts,tgd->sd/dot_general | solution.py:43
  143.2 0.0 reduce-scatter.7.cloned.1.call-update
  143.2 0.0 reduce-scatter.11.cloned.1.call-start
  143.3 7.2 %convolution_bitcast_fusion.2 = f32[256,4,128]{2,0,1:T(8,128)S(1)} fusion(bf16[4,256,4096]{1,2,0:T(8,128)(2,1)} %copy-done.1, bf16[4096,1,128]{0,2,1:T(8,128)(2,1)} %all-gather.6.cloned.1.call-done), kind=kOutput, calls=%fused_computation.20 | convolution fusion | flops 1073741824 | bytes 9961472 | tf_op jit(solution)/shard_map/gts,sd->tgd/dot_general | solution.py:43
  150.5 0.3 subtract_convert_fusion
  150.8 0.1 pad_maximum_fusion.1
  150.9 0.1 copy.37
  151.1 46.3 %reduce-scatter.5.cloned.1.call-done = bf16[256,128]{0,1:T(8,128)(2,1)} async-done(((bf16[4096,128]{0,1:T(8,128)(2,1)}), bf16[256,128]{0,1:T(8,128)(2,1)}) %reduce-scatter.5.cloned.1.call-update) | async-done | bytes 65552 | tf_op jit(solution)/shard_map/reduce_scatter | solution.py:107
  197.3 0.8 bitcast_convert_fusion
  198.2 0.3 fusion.30
  198.5 68.9 %reduce-scatter.7.cloned.1.call-done = bf16[256,128]{1,0:T(8,128)(2,1)} async-done(((bf16[4096,128]{1,0:T(8,128)(2,1)}), bf16[256,128]{1,0:T(8,128)(2,1)}) %reduce-scatter.7.cloned.1.call-update) | async-done | bytes 65552 | tf_op jit(solution)/shard_map/reduce_scatter | solution.py:110
  267.5 0.9 copy.40
  268.4 4.5 %fusion.5 = bf16[4096,768]{0,1:T(8,128)(2,1)} fusion(bf16[256,4096]{1,0:T(8,128)(2,1)S(1)} %copy-done, bf16[256,128]{0,1:T(8,128)(2,1)S(1)} %copy.40, bf16[256,128]{0,1:T(8,128)(2,1)S(1)} %maximum_bitcast_fusion, bf16[256,512]{0,1:T(8,128)(2,1)S(1)} %bitcast.84), kind=kOutput, calls=%fused_computation.10 | convolution fusion | flops 1614938112 | bytes 8781824 | tf_op jit(solution)/shard_map/dot_general | solution.py:119
  272.9 0.0 reduce-scatter.11.cloned.1.call-update
  272.9 0.0 copy-start.3
  272.9 0.3 reduce-scatter.9.cloned.1.call-start
  273.2 2.0 fusion.50
  275.2 3.6 convolution_add_fusion
  278.9 2.1 fusion.6
  281.0 0.0 reduce-scatter.9.cloned.1.call-update
  281.0 80.8 %reduce-scatter.11.cloned.1.call-done = bf16[256,768]{0,1:T(8,128)(2,1)} async-done(((bf16[4096,768]{0,1:T(8,128)(2,1)}), bf16[256,768]{0,1:T(8,128)(2,1)}) %reduce-scatter.11.cloned.1.call-update) | async-done | bytes 393232 | tf_op jit(solution)/shard_map/reduce_scatter | solution.py:118
  361.8 1.0 slice.52
  362.8 1.0 copy.41
  363.8 0.9 fusion.54
  364.7 0.8 copy.42
  365.4 0.8 copy.43
  366.2 40.0 %reduce-scatter.9.cloned.1.call-done = bf16[256,512]{1,0:T(8,128)(2,1)} async-done(((bf16[256,4096]{1,0:T(8,128)(2,1)}), bf16[256,512]{1,0:T(8,128)(2,1)}) %reduce-scatter.9.cloned.1.call-update) | async-done | bytes 262160 | tf_op jit(solution)/shard_map/reduce_scatter | solution.py:141
  (25 shorter events, 0.1 us)
Async XLA Ops:
  7.2 1.6 copy-start
  7.2 50.2 %all-gather.6.cloned.1.call-start = ((), (), s32[]{:S(2)}) async-start(), calls=%async_computation.9 | async-start | bytes 1114112 | tf_op jit(solution)/shard_map/all_gather | solution.py:91
  7.2 9.1 %copy-start.11 = (f32[64]{0:T(128)}, f32[64]{0:T(128)S(1)}, u32[]{:S(2)}) copy-start(f32[64]{0:T(128)S(1)} %negate_power_fusion) | copy-start | bytes 772
  8.8 7.6 %copy-start.9 = (f32[256]{0:T(256)}, f32[256]{0:T(256)S(1)}, u32[]{:S(2)}) copy-start(f32[256]{0:T(256)S(1)} %convert_element_type.52) | copy-start | bytes 3076
  8.8 14.5 %copy-start.7 = (bf16[256,512]{1,0:T(8,128)(2,1)S(1)}, bf16[256,512]{1,0:T(8,128)(2,1)}, u32[]{:S(2)}) copy-start(bf16[256,512]{1,0:T(8,128)(2,1)} %param.13) | copy-start | bytes 786436
  11.9 92.9 %all-gather.4.cloned.1.call-start = ((), (), s32[]{:S(2)}) async-start(), calls=%async_computation.4 | async-start | bytes 1114112 | tf_op jit(solution)/shard_map/all_gather | solution.py:92
  14.5 182.9 %reduce-scatter.5.cloned.1.call-start = ((), (), s32[]{:S(2)}) async-start(), calls=%async_computation.5 | async-start | bytes 1114112 | tf_op jit(solution)/shard_map/reduce_scatter | solution.py:107
  61.8 5.7 %copy-start.2 = (f32[4096,256,4]{1,0,2:T(8,128)}, f32[4096,256,4]{1,0,2:T(8,128)S(1)}, u32[]{:S(2)}) copy-start(f32[4096,256,4]{1,0,2:T(8,128)S(1)} %get-tuple-element.28) | copy-start | bytes 50331652
  104.7 10.0 %copy-start.8 = (bf16[256,512]{0,1:T(8,128)(2,1)S(1)}, bf16[256,512]{0,1:T(8,128)(2,1)}, u32[]{:S(2)}) copy-start(bf16[256,512]{0,1:T(8,128)(2,1)} %copy.31) | copy-start | bytes 786436
  104.7 10.0 %copy-start.13 = (bf16[4096,128]{1,0:T(8,128)(2,1)S(1)}, bf16[4096,128]{1,0:T(8,128)(2,1)}, u32[]{:S(2)}) copy-start(bf16[4096,128]{1,0:T(8,128)(2,1)} %all-gather.4.cloned.1.call-done) | copy-start | bytes 3145732
  114.7 12.9 %copy-start.4 = (bf16[256,4,64]{2,0,1:T(8,128)(2,1)S(1)}, bf16[256,4,64]{2,0,1:T(8,128)(2,1)}, u32[]{:S(2)}) copy-start(bf16[256,4,64]{2,0,1:T(8,128)(2,1)} %get-tuple-element.13) | copy-start | bytes 393220
  124.4 3.2 copy-start.1
  131.5 135.9 %reduce-scatter.7.cloned.1.call-start = ((), (), s32[]{:S(2)}) async-start(), calls=%async_computation.6 | async-start | bytes 1114112 | tf_op jit(solution)/shard_map/reduce_scatter | solution.py:110
  143.2 7.3 %copy-start.5 = (f32[256,64]{1,0:T(8,128)S(1)}, f32[256,64]{1,0:T(8,128)}, u32[]{:S(2)}) copy-start(f32[256,64]{1,0:T(8,128)} %get-tuple-element.24) | copy-start | bytes 196612
  143.2 55.0 %copy-start.10 = (f32[256]{0:T(256)S(1)}, f32[256]{0:T(256)}, u32[]{:S(2)}) copy-start(f32[256]{0:T(256)} %copy-done.9) | copy-start | bytes 3076
  143.2 55.0 %copy-start.12 = (f32[64]{0:T(128)S(1)}, f32[64]{0:T(128)}, u32[]{:S(2)}) copy-start(f32[64]{0:T(128)} %copy-done.11) | copy-start | bytes 772
  143.2 218.6 %reduce-scatter.11.cloned.1.call-start = ((), (), s32[]{:S(2)}) async-start(), calls=%async_computation.8 | async-start | bytes 6684672 | tf_op jit(solution)/shard_map/reduce_scatter | solution.py:118
  272.9 5.9 %copy-start.3 = (bf16[4096,128]{1,0:T(8,128)(2,1)S(1)}, bf16[4096,128]{1,0:T(8,128)(2,1)}, u32[]{:S(2)}) copy-start(bf16[4096,128]{1,0:T(8,128)(2,1)} %param.10) | copy-start | bytes 3145732
  272.9 5.9 %copy-start.6 = (bf16[256,128]{1,0:T(8,128)(2,1)S(1)}, bf16[256,128]{1,0:T(8,128)(2,1)}, u32[]{:S(2)}) copy-start(bf16[256,128]{1,0:T(8,128)(2,1)} %reduce-scatter.7.cloned.1.call-done) | copy-start | bytes 196612
  272.9 133.3 %reduce-scatter.9.cloned.1.call-start = ((), (), s32[]{:S(2)}) async-start(), calls=%async_computation.7 | async-start | bytes 2359296 | tf_op jit(solution)/shard_map/reduce_scatter | solution.py:141
Sparse Core Ops, SparseCore 0:
  12.0 45.3 all-gather.5
  59.8 44.8 all-gather.3
  131.7 65.6 reduce-scatter.4
  201.4 65.9 reduce-scatter.6
  273.0 88.7 reduce-scatter.10
  364.8 41.4 reduce-scatter.8
where the time goes:
time: 414 us; the launch traced here: 413 us
  waiting for transfers between devices  302 us (73%)
  matrix products  66.8 us (16%)
  local copies, waits for them, and re-layouts  14.5 us (4%)
  other arithmetic  14.5 us (4%)
  between operations  14.4 us (3%)
    reduce_scatter x1, waiting for transfers between devices, body(): lax.psum_scatter(lax.dot_general(normed, joined, (((0,), (0,)), ((), ()))...  80.8 us
    reduce_scatter x1, waiting for transfers between devices, body(): lax.psum_scatter(grad_value.astype(jnp.bfloat16), 'seq', scatter_dimensio...  68.9 us
    dot_general x6, matrix products, product(): return jnp.einsum(form, left, right, preferred_element_type=jnp.float32)  46.6 us
    reduce_scatter x1, waiting for transfers between devices, body(): lax.psum_scatter(grad_key.astype(jnp.bfloat16), 'seq', scatter_dimension=...  46.3 us
    reduce_scatter x1, waiting for transfers between devices, body(): lax.psum_scatter(partial_input.astype(jnp.bfloat16), 'kvh', scatter_dimen...  40 us
    all_gather x1, waiting for transfers between devices, body(): lax.all_gather(values, 'seq', axis=0, tiled=True)  37.1 us
    all_gather x1, waiting for transfers between devices, body(): lax.all_gather(keys, 'seq', axis=0, tiled=True)  28.9 us
    unnamed x33, local copies, waits for them, and re-layouts  10 us
  transfers between devices with their start and end apart: 6, of which 6 were waited for; matrix products, arithmetic and copies ran while one was open for 14% of the time, Pallas kernels for 0%

commit v1 on v0

--- a/solution.py
+++ b/solution.py
@@ -89,7 +89,9 @@
     values = jnp.dot(normed, w_value, preferred_element_type=jnp.float32).astype(jnp.bfloat16)
     keys_all, values_all = (
         lax.all_gather(keys, "seq", axis=0, tiled=True),
-        lax.all_gather(values, "seq", axis=0, tiled=True),
+        jnp.concatenate(
+            lax.all_to_all(jnp.stack([values] * lax.axis_size("seq")), "seq", 0, 0), axis=0
+        ),
     )
     seen = visible(block_mask, my_index * blk_local, tok_rows, keys_all.shape[0])
     total_parts = []

time: 414 us -> 383 us (0.925)
  waiting for transfers between devices: 302 us -> 267 us
  starting transfers between devices: 0.73 us -> 8.47 us
    all_gather x1 -> x0, waiting for transfers between devices: 37.1 us -> none  [body(): lax.all_gather(values, 'seq', axis=0, tiled=True)]
    all_to_all x0 -> x1, starting transfers between devices: none -> 8.01 us  [body(): lax.all_to_all(jnp.stack([values] * lax.axis_size('seq')), 'seq', 0, 0)]
    unnamed x33 -> x27, local copies, waits for them, and re-layouts: 10 us -> 9.41 us
  transfers between devices with their start and end apart: 6 -> 6, of which waited for: 6 -> 5; matrix products, arithmetic and copies ran while one was open for 14% -> 14% of each run, Pallas kernels for 0% -> 0%
where the time goes in v1:
time: 383 us; the launch traced here: 382 us
  waiting for transfers between devices  267 us (70%)
  matrix products  67.1 us (18%)
  local copies, waits for them, and re-layouts  14.3 us (4%)
  between operations  14.1 us (4%)
  other arithmetic  11.8 us (3%)
  starting transfers between devices  8.47 us (2%)
    reduce_scatter x1, waiting for transfers between devices, body(): lax.psum_scatter(lax.dot_general(normed, joined, (((0,), (0,)), ((), ()))...  81.1 us
    reduce_scatter x1, waiting for transfers between devices, body(): lax.psum_scatter(grad_value.astype(jnp.bfloat16), 'seq', scatter_dimensio...  69.1 us
    reduce_scatter x1, waiting for transfers between devices, body(): lax.psum_scatter(grad_key.astype(jnp.bfloat16), 'seq', scatter_dimension=...  47.5 us
    dot_general x6, matrix products, product(): return jnp.einsum(form, left, right, preferred_element_type=jnp.float32)  47.5 us
    reduce_scatter x1, waiting for transfers between devices, body(): lax.psum_scatter(partial_input.astype(jnp.bfloat16), 'kvh', scatter_dimen...  40.1 us
    all_gather x1, waiting for transfers between devices, body(): lax.all_gather(keys, 'seq', axis=0, tiled=True)  28.9 us
    unnamed x27, local copies, waits for them, and re-layouts  9.41 us
    all_to_all x1, starting transfers between devices, body(): lax.all_to_all(jnp.stack([values] * lax.axis_size('seq')), 'seq', 0, 0)  8.01 us
  transfers between devices with their start and end apart: 6, of which 5 were waited for; matrix products, arithmetic and copies ran while one was open for 14% of the time, Pallas kernels for 0%

profile of v1, /device:TPU:0, one launch (start us, length us, event | category | flops | bytes accessed | tf_op | source)
XLA Modules:
  0.0 382.4 jit_solution(11888233251317039786)
XLA Ops:
  7.2 0.0 copy-start
  7.2 0.0 all-gather.3.cloned.1.call-start
  7.2 0.8 convert_element_type.52
  8.1 0.7 copy-done
  8.8 2.0 convolution_bitcast_fusion.3
  10.8 0.0 copy-start.10
  10.8 0.0 copy-start.8
  10.9 0.3 fusion.32
  11.2 0.6 pad_maximum_fusion.2
  11.8 0.0 all-gather.3.cloned.1.call-update
  11.8 1.9 convolution_convert_fusion.1
  13.8 1.2 stack.2
  15.0 8.0 %all-to-all-start = ((bf16[16,256,128]{2,1,0:T(8,128)(2,1)}), bf16[16,256,128]{2,1,0:T(8,128)(2,1)}, u32[]{:S(2)}, u32[]{:S(2)}) async-start(bf16[16,256,128]{2,1,0:T(8,128)(2,1)} %stack.2), calls=%async_computation | async-start | bytes 2097152 | tf_op jit(solution)/shard_map/all_to_all | solution.py:93
  23.0 0.0 reduce-scatter.5.cloned.1.call-start
  23.0 3.5 fusion.53
  26.5 0.2 reshape.298
  26.7 0.1 copy.27
  26.8 0.1 broadcast_in_dim.30
  27.0 0.8 copy.31
  27.8 2.7 bitcast_and_fusion
  30.5 1.2 broadcast_multiply_fusion
  31.7 0.3 fusion.51
  32.0 0.8 subtract_convert_fusion.1
  32.9 28.9 %all-gather.3.cloned.1.call-done = bf16[4096,1,128]{0,2,1:T(8,128)(2,1)} async-done(((bf16[256,1,128]{0,2,1:T(8,128)(2,1)}), bf16[4096,1,128]{0,2,1:T(8,128)(2,1)}) %all-gather.3.cloned.1.call-update) | async-done | bytes 1048592 | tf_op jit(solution)/shard_map/all_gather | solution.py:91
  61.7 4.9 %fusion.4 = (f32[4,256]{1,0:T(4,128)S(1)}, f32[4096,256,4]{1,0,2:T(8,128)S(1)}) fusion(pred[256,4096]{0,1:T(8,128)(4,1)} %bitcast_and_fusion, bf16[256,4,64]{2,0,1:T(8,128)(2,1)} %get-tuple-element.13, bf16[256,4,64]{2,0,1:T(8,128)(2,1)S(1)} %get-tuple-element.12, bf16[4096,1,128]{0,2,1:T(8,128)(2,1)} %all-gather.3.cloned.1.call-done), kind=kOutput, calls=%fused_computation.8 | convolution fusion | flops 1086848000 | bytes 19140608 | tf_op jit(solution)/shard_map/tgd,sd->gts/dot_general | solution.py:43
  66.7 3.7 exponential_reduce_fusion
  70.3 2.1 copy-done.2
  72.4 0.0 all-to-all-done
  72.4 0.0 copy-start.9
  72.4 10.0 %fusion.9 = f32[4,256]{1,0:T(4,128)S(1)} fusion(bf16[4096,128,1]{1,0,2:T(8,128)(2,1)} %bitcast.7, bf16[256,4,128]{0,2,1:T(8,128)(2,1)} %bitcast.86, f32[4096,256,4]{1,0,2:T(8,128)} %copy-done.2, f32[4,256]{1,0:T(4,128)S(1)} %log_add_fusion, pred[256,4096]{0,1:T(8,128)(4,1)S(1)} %copy-done.4), kind=kOutput, calls=%fused_computation.21 | convolution fusion | flops 1095105536 | bytes 19144704 | tf_op jit(solution)/shard_map/gts,sd->gtd/dot_general | solution.py:43
  82.4 0.0 copy-start.5
  82.4 10.1 %fusion.2 = bf16[4,256,4096]{1,2,0:T(8,128)(2,1)S(1)} fusion(f32[4096,256,4]{1,0,2:T(8,128)} %copy-done.2, bf16[4096,128,1]{1,0,2:T(8,128)(2,1)} %bitcast.7, bf16[256,4,128]{0,2,1:T(8,128)(2,1)S(1)} %bitcast.88, f32[4,256]{1,0:T(4,128)S(1)} %fusion.9, f32[4,256]{1,0:T(4,128)S(1)} %log_add_fusion, pred[256,4096]{0,1:T(8,128)(4,1)S(1)} %copy-done.4), kind=kOutput, calls=%fused_computation.3 | convolution fusion | flops 1107296256 | bytes 27533312 | tf_op jit(solution)/shard_map/tgd,sd->gts/dot_general | solution.py:43
  92.5 3.2 copy-done.1
  95.7 3.9 %fusion.7 = bf16[4096,128]{0,1:T(8,128)(2,1)} fusion(bf16[4,256,4096]{1,2,0:T(8,128)(2,1)S(1)} %fusion.2, bf16[256,4,64]{2,0,1:T(8,128)(2,1)S(1)} %copy-done.5, bf16[256,4,64]{2,0,1:T(8,128)(2,1)S(1)} %get-tuple-element.12), kind=kOutput, calls=%fused_computation.16 | convolution fusion | flops 1074790400 | bytes 9699328 | tf_op jit(solution)/shard_map/gts,tgd->sd/dot_general | solution.py:43
  99.6 0.0 reduce-scatter.5.cloned.1.call-update
  99.6 0.0 reduce-scatter.7.cloned.1.call-start
  99.7 11.4 %fusion.8 = bf16[4096,128]{1,0:T(8,128)(2,1)} fusion(bf16[256,4,128]{0,2,1:T(8,128)(2,1)} %bitcast.87, f32[4096,256,4]{1,0,2:T(8,128)} %copy-done.2, f32[4,256]{1,0:T(4,128)S(1)} %log_add_fusion, pred[256,4096]{0,1:T(8,128)(4,1)S(1)} %copy-done.4), kind=kOutput, calls=%fused_computation.17 | convolution fusion | flops 1095237632 | bytes 19140608 | tf_op jit(solution)/shard_map/gts,tgd->sd/dot_general | solution.py:43
  111.1 0.0 reduce-scatter.7.cloned.1.call-update
  111.1 0.3 reduce-scatter.11.cloned.1.call-start
  111.4 7.2 %convolution_bitcast_fusion.2 = f32[256,4,128]{2,0,1:T(8,128)S(1)} fusion(bf16[4,256,4096]{1,2,0:T(8,128)(2,1)} %copy-done.1, bf16[4096,1,128]{0,2,1:T(8,128)(2,1)} %all-gather.3.cloned.1.call-done), kind=kOutput, calls=%fused_computation.20 | convolution fusion | flops 1073741824 | bytes 9961472 | tf_op jit(solution)/shard_map/gts,sd->tgd/dot_general | solution.py:43
  118.7 0.3 subtract_convert_fusion
  118.9 0.1 pad_maximum_fusion.1
  119.1 0.1 copy.37
  119.2 47.5 %reduce-scatter.5.cloned.1.call-done = bf16[256,128]{0,1:T(8,128)(2,1)} async-done(((bf16[4096,128]{0,1:T(8,128)(2,1)}), bf16[256,128]{0,1:T(8,128)(2,1)}) %reduce-scatter.5.cloned.1.call-update) | async-done | bytes 65552 | tf_op jit(solution)/shard_map/reduce_scatter | solution.py:109
  166.7 0.8 bitcast_convert_fusion
  167.6 0.3 fusion.28
  167.9 69.1 %reduce-scatter.7.cloned.1.call-done = bf16[256,128]{1,0:T(8,128)(2,1)} async-done(((bf16[4096,128]{1,0:T(8,128)(2,1)}), bf16[256,128]{1,0:T(8,128)(2,1)}) %reduce-scatter.7.cloned.1.call-update) | async-done | bytes 65552 | tf_op jit(solution)/shard_map/reduce_scatter | solution.py:112
  237.0 0.9 copy.40
  238.0 4.5 %fusion.5 = bf16[4096,768]{0,1:T(8,128)(2,1)} fusion(bf16[256,4096]{1,0:T(8,128)(2,1)S(1)} %copy-done, bf16[256,128]{0,1:T(8,128)(2,1)S(1)} %copy.40, bf16[256,128]{0,1:T(8,128)(2,1)S(1)} %maximum_bitcast_fusion, bf16[256,512]{0,1:T(8,128)(2,1)S(1)} %bitcast.84), kind=kOutput, calls=%fused_computation.10 | convolution fusion | flops 1614938112 | bytes 8781824 | tf_op jit(solution)/shard_map/dot_general | solution.py:121
  242.4 0.0 reduce-scatter.11.cloned.1.call-update
  242.5 0.0 copy-start.3
  242.5 0.0 copy-start.7
  242.5 0.0 reduce-scatter.9.cloned.1.call-start
  242.5 2.0 fusion.48
  244.6 3.6 convolution_add_fusion
  248.2 2.1 fusion.6
  250.3 0.0 reduce-scatter.9.cloned.1.call-update
  250.3 81.1 %reduce-scatter.11.cloned.1.call-done = bf16[256,768]{0,1:T(8,128)(2,1)} async-done(((bf16[4096,768]{0,1:T(8,128)(2,1)}), bf16[256,768]{0,1:T(8,128)(2,1)}) %reduce-scatter.11.cloned.1.call-update) | async-done | bytes 393232 | tf_op jit(solution)/shard_map/reduce_scatter | solution.py:120
  331.4 1.0 slice.52
  332.4 1.0 copy.41
  333.4 0.9 fusion.52
  334.3 0.8 copy.42
  335.0 0.8 copy.43
  335.8 40.1 %reduce-scatter.9.cloned.1.call-done = bf16[256,512]{1,0:T(8,128)(2,1)} async-done(((bf16[256,4096]{1,0:T(8,128)(2,1)}), bf16[256,512]{1,0:T(8,128)(2,1)}) %reduce-scatter.9.cloned.1.call-update) | async-done | bytes 262160 | tf_op jit(solution)/shard_map/reduce_scatter | solution.py:143
  (19 shorter events, 0.1 us)
Async XLA Ops:
  7.2 1.6 copy-start
  7.2 54.5 %all-gather.3.cloned.1.call-start = ((), (), s32[]{:S(2)}) async-start(), calls=%async_computation.9 | async-start | bytes 1114112 | tf_op jit(solution)/shard_map/all_gather | solution.py:91
  10.8 15.9 %copy-start.10 = (s32[2,32]{1,0:T(2,128)S(1)}, s32[2,32]{1,0:T(2,128)}, u32[]{:S(2)}) copy-start(s32[2,32]{1,0:T(2,128)} %param.12) | copy-start | bytes 772
  10.8 16.1 %copy-start.8 = (bf16[256,512]{1,0:T(8,128)(2,1)S(1)}, bf16[256,512]{1,0:T(8,128)(2,1)}, u32[]{:S(2)}) copy-start(bf16[256,512]{1,0:T(8,128)(2,1)} %param.13) | copy-start | bytes 786436
  15.0 57.4 %all-to-all-start = ((bf16[16,256,128]{2,1,0:T(8,128)(2,1)}), bf16[16,256,128]{2,1,0:T(8,128)(2,1)}, u32[]{:S(2)}, u32[]{:S(2)}) async-start(bf16[16,256,128]{2,1,0:T(8,128)(2,1)} %stack.2), calls=%async_computation | async-start | bytes 2097152 | tf_op jit(solution)/shard_map/all_to_all | solution.py:93
  23.0 143.7 %reduce-scatter.5.cloned.1.call-start = ((), (), s32[]{:S(2)}) async-start(), calls=%async_computation.5 | async-start | bytes 1114112 | tf_op jit(solution)/shard_map/reduce_scatter | solution.py:109
  61.7 4.9 %copy-start.4 = (pred[256,4096]{0,1:T(8,128)(4,1)S(1)}, pred[256,4096]{0,1:T(8,128)(4,1)}, u32[]{:S(2)}) copy-start(pred[256,4096]{0,1:T(8,128)(4,1)} %bitcast_and_fusion) | copy-start | bytes 3145732
  66.6 5.7 %copy-start.2 = (f32[4096,256,4]{1,0,2:T(8,128)}, f32[4096,256,4]{1,0,2:T(8,128)S(1)}, u32[]{:S(2)}) copy-start(f32[4096,256,4]{1,0,2:T(8,128)S(1)} %get-tuple-element.28) | copy-start | bytes 50331652
  72.4 10.0 %copy-start.9 = (bf16[256,512]{0,1:T(8,128)(2,1)S(1)}, bf16[256,512]{0,1:T(8,128)(2,1)}, u32[]{:S(2)}) copy-start(bf16[256,512]{0,1:T(8,128)(2,1)} %copy.31) | copy-start | bytes 786436
  82.4 13.3 %copy-start.5 = (bf16[256,4,64]{2,0,1:T(8,128)(2,1)S(1)}, bf16[256,4,64]{2,0,1:T(8,128)(2,1)}, u32[]{:S(2)}) copy-start(bf16[256,4,64]{2,0,1:T(8,128)(2,1)} %get-tuple-element.13) | copy-start | bytes 393220
  92.5 3.2 copy-start.1
  99.6 137.4 %reduce-scatter.7.cloned.1.call-start = ((), (), s32[]{:S(2)}) async-start(), calls=%async_computation.6 | async-start | bytes 1114112 | tf_op jit(solution)/shard_map/reduce_scatter | solution.py:112
  111.1 7.6 %copy-start.6 = (f32[256,64]{1,0:T(8,128)S(1)}, f32[256,64]{1,0:T(8,128)}, u32[]{:S(2)}) copy-start(f32[256,64]{1,0:T(8,128)} %get-tuple-element.24) | copy-start | bytes 196612
  111.1 220.3 %reduce-scatter.11.cloned.1.call-start = ((), (), s32[]{:S(2)}) async-start(), calls=%async_computation.8 | async-start | bytes 6684672 | tf_op jit(solution)/shard_map/reduce_scatter | solution.py:120
  242.5 5.7 %copy-start.3 = (bf16[4096,128]{1,0:T(8,128)(2,1)S(1)}, bf16[4096,128]{1,0:T(8,128)(2,1)}, u32[]{:S(2)}) copy-start(bf16[4096,128]{1,0:T(8,128)(2,1)} %param.10) | copy-start | bytes 3145732
  242.5 5.7 %copy-start.7 = (bf16[256,128]{1,0:T(8,128)(2,1)S(1)}, bf16[256,128]{1,0:T(8,128)(2,1)}, u32[]{:S(2)}) copy-start(bf16[256,128]{1,0:T(8,128)(2,1)} %reduce-scatter.7.cloned.1.call-done) | copy-start | bytes 196612
  242.5 133.4 %reduce-scatter.9.cloned.1.call-start = ((), (), s32[]{:S(2)}) async-start(), calls=%async_computation.7 | async-start | bytes 2359296 | tf_op jit(solution)/shard_map/reduce_scatter | solution.py:143
Sparse Core Ops, SparseCore 0:
  12.0 49.7 all-gather.2
  99.8 66.9 reduce-scatter.4
  171.0 65.9 reduce-scatter.6
  242.6 88.7 reduce-scatter.10
  334.3 41.4 reduce-scatter.8
